TPU v7x, 32 devices: a whole 2x2x4 slice. The times are simulated.
32 devices in a mesh: freq: 2 (over y), gx: 4 (over z), gy: 2 (over x), col: 2 (over core).
Axes of the slice: x: 2, y: 2, z: 4, core: 2. Of those that a mesh axis runs over, the one named last changes fastest.
Arguments:
- source: bfloat16 [12, 64, 32, 256], P('freq', 'gx', 'gy', 'col'), parts along dimension 0, may hold values from -6 to 6
- warm: bfloat16 [12, 64, 32, 256], P('freq', 'gx', 'gy', 'col'), parts along dimension 0, may hold values from -2.1 to 2.6
- forward: bfloat16 [12, 64, 32, 256], P('freq', 'gx', 'gy', 'col'), parts along dimension 0, may hold values from -6 to 6
- density: bfloat16 [64, 32, 256], P('gx', 'gy', 'col'), may hold values from 1 to 3
- material_map: int32 [8, 4, 8], P('gx', 'gy', 'col'), may hold values from 0 to 7
- material_table: float32 [8, 2], replicated, may hold values from 0.5 to 2
- iface_cells: int32 [16, 256], P(('gx', 'gy', 'col')), may hold values from 0 to 32767, as said below
- impedance: float32 [2, 3], replicated, may hold values from 2 to 8
- omega2: float32 [2], P('freq'), parts along dimension 0, may hold values from 0.5 to 1
Outputs:
- adjoint: float32 [12, 64, 32, 256], P('freq', 'gx', 'gy', 'col'), parts along dimension 0
- coarse_gradient: float32 [32, 8], P('freq'), parts along dimension 0
There are 2 independent parts, one for each index of `freq`. A program takes and returns all parts, laid end to end along the dimension named above; an argument that names none is the same for every part. Nothing has to cross between parts.
Inputs may be any that keep to these rules, and one draw needn't show every extreme that they name: `iface_cells`: each row's entries are distinct, rising, and within the tile of 16 x 16 x 128 cells; row r belongs to the device of that index along gx, gy and col together.
All inputs are finite; a program needn't handle non-finite values.
Results may differ from a plain program's by a relative error of at most 0.0003.
Values may be sent and summed in bfloat16 or wider, within the bound.
No kernel may reach another device: no remote copies, remote signals or barrier semaphores. Data moves between devices by JAX's collectives and lax.ppermute only.
A program may use at most 64 MiB of HBM per device.

v0:
```python
import jax
import jax.numpy as jnp
from jax import lax
from jax.sharding import PartitionSpec as P

DAMPING = 0.5
RELAXATION = 0.6


def with_halo(array, sides, width):
    for axis, dim in sides:
        peers, length = (lax.axis_size(axis), array.shape[dim])
        up = [(i, (i + 1) % peers) for i in range(peers - 1)]
        down = [(j, i) for i, j in up]
        last = lax.slice_in_dim(array, length - width, length, axis=dim)
        initial = lax.slice_in_dim(array, 0, width, axis=dim)
        before = lax.ppermute(last, axis, up)
        after = lax.ppermute(initial, axis, down)
        array = jnp.concatenate([before, array, after], axis=dim)
    return array


def window(padded, offset):
    size_x = padded.shape[1] - 2
    size_y = padded.shape[2] - 2
    size_z = padded.shape[3] - 2
    return padded[
        :,
        1 + offset[0] : 1 + offset[0] + size_x,
        1 + offset[1] : 1 + offset[1] + size_y,
        1 + offset[2] : 1 + offset[2] + size_z,
    ]


def navier(padded, lame_first, shear):
    units = ((1, 0, 0), (0, 1, 0), (0, 0, 1))
    centre = window(padded, (0, 0, 0))
    second = []
    for axis_d in range(3):
        ahead = units[axis_d]
        behind = tuple((-value for value in ahead))
        second.append(window(padded, ahead) + window(padded, behind) - 2.0 * centre)
    laplace = second[0] + second[1] + second[2]
    result = []
    for part_index in range(2):
        for component in range(3):
            channel = part_index * 3 + component
            divergence = second[component][channel]
            for other_axis in range(3):
                if other_axis != component:
                    source_channel = part_index * 3 + other_axis
                    single = padded[source_channel : source_channel + 1]
                    first_unit = units[component]
                    other_unit = units[other_axis]
                    plus_plus = tuple((first_unit[k] + other_unit[k] for k in range(3)))
                    plus_minus = tuple((first_unit[k] - other_unit[k] for k in range(3)))
                    minus_plus = tuple((-first_unit[k] + other_unit[k] for k in range(3)))
                    minus_minus = tuple((-first_unit[k] - other_unit[k] for k in range(3)))
                    mixed = (
                        window(single, plus_plus)
                        - window(single, plus_minus)
                        - window(single, minus_plus)
                        + window(single, minus_minus)
                    )
                    divergence = divergence + 0.25 * mixed[0]
            result.append(shear * laplace[channel] + (lame_first + shear) * divergence)
    return jnp.stack(result)


def sweep(padded, lame_first, shear, density, mask, source, mean_field, omega_sq, impedance):
    field = window(padded, (0, 0, 0))
    elastic = navier(padded, lame_first, shear)
    real_part = field[:3]
    imag_part = field[3:]
    mean_real = mean_field[:3][:, None, None, None]
    mean_imag = mean_field[3:][:, None, None, None]
    imp_real = impedance[0][:, None, None, None]
    imp_imag = impedance[1][:, None, None, None]
    inertia = omega_sq * density
    diff_real = real_part - mean_real
    diff_imag = imag_part - mean_imag
    apply_real = (
        -elastic[:3]
        - inertia * (real_part - DAMPING * imag_part)
        + mask * (imp_real * diff_real - imp_imag * diff_imag)
    )
    apply_imag = (
        -elastic[3:]
        - inertia * (imag_part + DAMPING * real_part)
        + mask * (imp_real * diff_imag + imp_imag * diff_real)
    )
    resid_real = source[:3] - apply_real
    resid_imag = source[3:] - apply_imag
    diag_real = 8.0 * shear + 2.0 * lame_first - inertia + mask * imp_real
    diag_imag = -DAMPING * inertia + mask * imp_imag
    modulus = diag_real * diag_real + diag_imag * diag_imag
    new_real = real_part + RELAXATION * (resid_real * diag_real + resid_imag * diag_imag) / modulus
    new_imag = imag_part + RELAXATION * (resid_imag * diag_real - resid_real * diag_imag) / modulus
    return jnp.concatenate([new_real, new_imag], 0)


def expand(blocks):
    blocks_x, blocks_y, blocks_z = blocks.shape
    spread = jnp.broadcast_to(
        blocks[:, None, :, None, :, None], (blocks_x, 8, blocks_y, 8, blocks_z, 32)
    )
    return spread.reshape(blocks_x * 8, blocks_y * 8, blocks_z * 32)


def material(block_ids, table):
    lame_first = jnp.zeros(block_ids.shape, jnp.float32)
    shear = jnp.zeros(block_ids.shape, jnp.float32)
    for entry in range(table.shape[0]):
        chosen = block_ids == entry
        lame_first = jnp.where(chosen, table[entry, 0], lame_first)
        shear = jnp.where(chosen, table[entry, 1], shear)
    return (lame_first, shear)


def foundation(field, mask, count):
    total = lax.psum(jnp.sum(mask * field, axis=(1, 2, 3)), ("gx", "gy", "col"))
    return total / count


def shards(
    source, warm, forward, density, material_map, material_table, iface_cells, impedance, omega2
):
    omega_sq = omega2[0]
    tile_shape = density.shape
    tile_cells = tile_shape[0] * tile_shape[1] * tile_shape[2]
    mask = jnp.zeros((tile_cells,), jnp.float32).at[iface_cells[0]].set(1.0).reshape(tile_shape)
    block_ids = expand(material_map)
    lame_first, shear = material(block_ids, material_table)
    density_cells = density.astype(jnp.float32)
    source_cells = source.astype(jnp.float32)
    group_size = lax.axis_size("gx") * lax.axis_size("gy") * lax.axis_size("col")
    count = jnp.float32(group_size * iface_cells.shape[1])
    field = warm.astype(jnp.float32)
    for sweep_index in range(2):
        mean_field = foundation(field, mask, count)
        padded = with_halo(field, (("gx", 1), ("gy", 2), ("col", 3)), 1)
        field = sweep(
            padded,
            lame_first,
            shear,
            density_cells,
            mask,
            source_cells,
            mean_field,
            omega_sq,
            impedance,
        )
    forward_cells = forward.astype(jnp.float32)
    correlation = (
        field[:3] * forward_cells[:3]
        - field[3:] * forward_cells[3:]
        - DAMPING * (field[:3] * forward_cells[3:] + field[3:] * forward_cells[:3])
    )
    cell_terms = -omega_sq * jnp.sum(correlation, axis=0)
    coarse_x = tile_shape[0] // 4
    coarse_y = tile_shape[1] // 4
    local_sums = cell_terms.reshape(coarse_x, 4, coarse_y, 4, tile_shape[2]).sum(axis=(1, 3, 4))
    paired = lax.psum(local_sums, "col")
    gathered = lax.all_gather(paired[None], ("gx", "gy"), axis=0, tiled=True)
    grid_sums = gathered.reshape(lax.axis_size("gx"), lax.axis_size("gy"), coarse_x, coarse_y)
    coarse = (
        grid_sums.transpose(0, 2, 1, 3).reshape(
            lax.axis_size("gx") * coarse_x, lax.axis_size("gy") * coarse_y
        )
        / 64.0
    )
    return (field, coarse)


def solution(mesh):
    in_specs = (
        P("freq", "gx", "gy", "col"),
        P("freq", "gx", "gy", "col"),
        P("freq", "gx", "gy", "col"),
        P("gx", "gy", "col"),
        P("gx", "gy", "col"),
        P(),
        P(("gx", "gy", "col"), None),
        P(),
        P("freq"),
    )
    out_specs = (P("freq", "gx", "gy", "col"), P("freq", None))
    return jax.shard_map(shards, mesh=mesh, in_specs=in_specs, out_specs=out_specs, check_vma=False)
```

profile of v0, /device:TPU:0, one launch (start us, length us, event | category | flops | bytes accessed | tf_op | source)
XLA Modules:
  0.0 208.3 jit_solution(2462226845284078183)
XLA Ops:
  0.6 0.8 fusion.107
  1.4 1.3 collective-permute-start
  2.7 5.6 %collective-permute-start.1 = (f32[6,1,16,128]{3,2,1,0:T(8,128)S(1)}, f32[6,1,16,128]{3,2,1,0:T(8,128)S(1)}, u32[]{:S(2)}, u32[]{:S(2)}) collective-permute-start(f32[6,1,16,128]{3,2,1,0:T(8,128)S(1)} %get-tuple-element.40), channel_id=1, source_target_pairs={{0,4},{4,8},{8,12},{1,5},{5,9},{9,13},{2,6},{6,10},{10,14},{3,7},{... | collective-permute-start | bytes 147464 | tf_op jit(solution)/shard_map/ppermute | solution.py:17
  8.3 2.0 fusion.108
  10.3 0.7 broadcast_compare_fusion.7
  11.0 1.9 broadcast_select_fusion
  12.9 4.6 %select_select_fusion.1 = f32[2,8,2,8,4,32]{5,4,3,2,1,0:T(4,128)S(1)} fusion(f32[]{:T(128)} %bitcast, f32[]{:T(128)} %bitcast.1, f32[]{:T(128)} %bitcast.2, f32[]{:T(128)} %bitcast.3, f32[]{:T(128)} %bitcast.4, f32[2,2,4]{2,1,0:T(2,128)S(1)} %get-tuple-element.46, f32[]{:T(128)} %bitcast.6, f32[]{:T(128)} %bitcast.5, ...), kind=kLoop, calls=%fused_computation.41 | loop fusion | flops 229376 | bytes 131276 | tf_op jit(solution)/shard_map/jit(_where)/select_n | solution.py:116
  17.4 4.5 %select_select_fusion = f32[2,8,2,8,4,32]{5,4,3,2,1,0:T(4,128)S(1)} fusion(f32[]{:T(128)} %bitcast.8, f32[]{:T(128)} %bitcast.9, f32[]{:T(128)} %bitcast.10, f32[]{:T(128)} %bitcast.11, f32[]{:T(128)} %bitcast.12, f32[2,2,4]{2,1,0:T(2,128)S(1)} %get-tuple-element.45, f32[]{:T(128)} %bitcast.14, f32[]{:T(128)} %bitcast.13, ...), kind=kLoop, calls=%fused_computation.40 | loop fusion | flops 229376 | bytes 131276 | tf_op jit(solution)/shard_map/jit(_where)/select_n | solution.py:115
  22.0 8.9 %multiply_add_fusion = f32[2,8,2,8,4,32]{5,4,3,2,1,0:T(4,128)S(1)} fusion(f32[2,2,4]{2,1,0:T(2,128)S(1)} %get-tuple-element.46, f32[]{:T(128)} %bitcast.6, pred[2,2,4]{2,1,0:T(4,128)(4,1)S(1)} %get-tuple-element.53, f32[]{:T(128)} %bitcast.5, pred[2,2,4]{2,1,0:T(4,128)(4,1)S(1)} %get-tuple-element.48, f32[]{:T(128)} %bitcast.4, ...), kind=kLoop, calls=%fused_computation.39 | loop fusion | flops 557056 | bytes 131368 | tf_op jit(solution)/shard_map/add | solution.py:94
  31.8 0.8 convert_multiply_fusion
  32.8 1.3 collective-permute-start.2
  34.1 5.8 %collective-permute-start.3 = (f32[6,18,1,128]{3,2,1,0:T(1,128)S(1)}, f32[6,18,1,128]{3,2,1,0:T(1,128)}, u32[]{:S(2)}, u32[]{:S(2)}) collective-permute-start(f32[6,18,1,128]{3,2,1,0:T(1,128)S(1)} %get-tuple-element.34), channel_id=1, source_target_pairs={{0,2},{1,3},{4,6},{5,7},{8,10},{9,11},{12,14},{13,15},{16,18},{17,... | collective-permute-start | bytes 165896 | tf_op jit(solution)/shard_map/ppermute | solution.py:17
  39.9 0.9 reshape.313
  40.8 0.9 reshape.315
  41.7 1.0 convert_element_type.13
  42.7 2.0 scatter_custom_fusion
  44.7 1.0 pad_maximum_fusion.3
  45.8 0.4 fusion.106
  46.2 1.6 copy.44
  47.8 1.3 collective-permute-start.4
  49.1 0.9 copy.46
  50.0 3.6 %collective-permute-start.5 = (f32[6,18,18,1]{2,1,3,0:T(8,128)S(1)}, f32[6,18,18,1]{2,1,3,0:T(8,128)}, u32[]{:S(2)}, u32[]{:S(2)}) collective-permute-start(f32[6,18,18,1]{2,1,3,0:T(8,128)S(1)} %copy.46), channel_id=1, source_target_pairs={{0,1},{2,3},{4,5},{6,7},{8,9},{10,11},{12,13},{14,15},{16,17},{18,... | collective-permute-start | bytes 23336 | tf_op jit(solution)/shard_map/ppermute | solution.py:17
  53.7 2.6 %pad_maximum_fusion.2 = (f32[6,18,17,128]{3,2,1,0:T(8,128)}, f32[6,18,17,128]{3,2,1,0:T(8,128)}) fusion(f32[6,18,1,128]{3,2,1,0:T(1,128)} %collective-permute-done.2, f32[6,1,16,128]{3,2,1,0:T(8,128)S(1)} %collective-permute-done, f32[6,16,16,128]{3,2,1,0:T(8,128)S(1)} %convert_element_type.12, f32[6,1,16,128]{3,2,1,0:T(8,128)S(1)} %collective-permute-done.1, ...), kind=kLoop, calls=%fused_computation.5 | loop fusion | flops 1410048 | bytes 2875392 | tf_op jit(solution)/shard_map/concatenate | solution.py:19
  56.2 0.8 copy.45
  57.0 1.7 copy.47
  58.7 3.1 %pad_maximum_fusion = (f32[6,18,18,129]{3,2,1,0:T(8,128)S(1)}, f32[6,18,18,129]{3,2,1,0:T(8,128)S(1)}) fusion(f32[6,18,18,1]{3,2,1,0:T(8,128)S(1)} %copy.45, f32[6,18,1,128]{3,2,1,0:T(1,128)} %collective-permute-done.2, f32[6,1,16,128]{3,2,1,0:T(8,128)S(1)} %collective-permute-done, f32[6,16,16,128]{3,2,1,0:T(8,128)S(1)} %convert_element_type.12, ...), kind=kLoop, calls=%fused_computation.1 | loop fusion | flops 2507760 | bytes 3017088 | tf_op jit(solution)/shard_map/concatenate | solution.py:19
  61.8 2.3 %add_add_fusion.1 = (f32[6,16,16,128]{3,2,1,0:T(8,128)}, f32[6,16,16,128]{3,2,1,0:T(8,128)}, f32[6,16,16,128]{3,2,1,0:T(8,128)}, f32[6,16,16,128]{3,2,1,0:T(8,128)}, f32[6]{0:T(128)S(1)}) fusion(bf16[6,16,16,128]{3,2,1,0:T(8,128)(2,1)S(1)} %copy-done.28, f32[6,18,17,128]{3,2,1,0:T(8,128)S(1)} %copy-done.17, f32[6,18,17,128]{3,2,1,0:T(8,128)S(1)} %copy-done.16, ...), kind=kLoop, calls=%fused_computation.38 | loop fusion | flops 2949114 | bytes 7700504 | tf_op jit(solution)/shard_map/add | solution.py:43
  64.2 29.5 %psum.21 = f32[6]{0:T(128)S(1)} all-reduce(f32[6]{0:T(128)S(1)} %get-tuple-element.39), channel_id=1, replica_groups=mesh['freq'=2,'gx'=4,'gy'=2,'col'=2] {'gx','gy','col'}, use_global_device_ids=true, to_apply=%region_2.3 | all-reduce | flops 6 | bytes 48 | tf_op jit(solution)/shard_map/psum | solution.py:121
  93.7 1.6 fusion.71
  95.4 1.4 fusion.89
  96.8 1.4 fusion.83
  98.3 1.4 fusion.65
  99.7 1.7 fusion.77
  101.5 1.7 fusion.59
  103.3 0.5 divide_add_fusion.3
  104.1 1.4 collective-permute-start.6
  105.5 4.5 %collective-permute-start.7 = (f32[6,1,16,128]{3,2,1,0:T(8,128)S(1)}, f32[6,1,16,128]{3,2,1,0:T(8,128)S(1)}, u32[]{:S(2)}, u32[]{:S(2)}) collective-permute-start(f32[6,1,16,128]{3,2,1,0:T(8,128)S(1)} %get-tuple-element.37), channel_id=1, source_target_pairs={{0,4},{4,8},{8,12},{1,5},{5,9},{9,13},{2,6},{6,10},{10,14},{3,7},{... | collective-permute-start | bytes 147464 | tf_op jit(solution)/shard_map/ppermute | solution.py:17
  110.2 1.6 collective-permute-done.7
  111.9 1.3 collective-permute-start.8
  113.2 4.7 %collective-permute-start.9 = (f32[6,18,1,128]{3,2,1,0:T(1,128)S(1)}, f32[6,18,1,128]{3,2,1,0:T(1,128)S(1)}, u32[]{:S(2)}, u32[]{:S(2)}) collective-permute-start(f32[6,18,1,128]{3,2,1,0:T(1,128)S(1)} %get-tuple-element.30), channel_id=1, source_target_pairs={{0,2},{1,3},{4,6},{5,7},{8,10},{9,11},{12,14},{13,15},{16,18},{17,... | collective-permute-start | bytes 165896 | tf_op jit(solution)/shard_map/ppermute | solution.py:17
  118.0 1.0 convert_element_type.15
  118.9 0.6 collective-permute-done.9
  119.6 0.6 copy-done.13
  120.8 1.6 copy.48
  122.4 1.4 collective-permute-start.10
  123.8 0.9 copy.50
  124.8 3.6 %collective-permute-start.11 = (f32[6,18,18,1]{2,1,3,0:T(8,128)S(1)}, f32[6,18,18,1]{2,1,3,0:T(8,128)}, u32[]{:S(2)}, u32[]{:S(2)}) collective-permute-start(f32[6,18,18,1]{2,1,3,0:T(8,128)S(1)} %copy.50), channel_id=1, source_target_pairs={{0,1},{2,3},{4,5},{6,7},{8,9},{10,11},{12,13},{14,15},{16,17},{18,... | collective-permute-start | bytes 23336 | tf_op jit(solution)/shard_map/ppermute | solution.py:17
  128.4 1.7 pad_maximum_fusion.4
  130.2 0.8 copy.49
  130.9 1.7 copy.51
  132.6 3.6 %pad_maximum_fusion.1 = (f32[6,18,18,129]{3,2,1,0:T(8,128)S(1)}, f32[6,18,18,129]{3,2,1,0:T(8,128)S(1)}) fusion(f32[6,18,18,1]{3,2,1,0:T(8,128)S(1)} %copy.49, f32[6,18,1,128]{3,2,1,0:T(1,128)} %copy-done.10, f32[6,1,16,128]{3,2,1,0:T(8,128)S(1)} %collective-permute-done.6, f32[3,16,16,128]{3,2,1,0:T(8,128)S(1)} %divide_add_fusion.2, ...), kind=kLoop, calls=%fused_computation.3 | loop fusion | flops 3009312 | bytes 3017088 | tf_op jit(solution)/shard_map/concatenate | solution.py:19
  136.3 2.3 %add_add_fusion = (f32[6,16,16,128]{3,2,1,0:T(8,128)}, f32[6,16,16,128]{3,2,1,0:T(8,128)}, f32[6,16,16,128]{3,2,1,0:T(8,128)}, f32[6,16,16,128]{3,2,1,0:T(8,128)}, f32[6]{0:T(128)S(1)}) fusion(f32[3,16,16,128]{3,2,1,0:T(8,128)S(1)} %divide_add_fusion.2, f32[3,16,16,128]{3,2,1,0:T(8,128)S(1)} %get-tuple-element.11, f32[6,18,17,128]{3,2,1,0:T(8,128)S(1)} %copy-done.19, ...), kind=kLoop, calls=%fused_computation.36 | loop fusion | flops 3145722 | bytes 7307288 | tf_op jit(solution)/shard_map/add | solution.py:43
  138.6 29.5 %psum.22 = f32[6]{0:T(128)S(1)} all-reduce(f32[6]{0:T(128)S(1)} %get-tuple-element.36), channel_id=1, replica_groups=mesh['freq'=2,'gx'=4,'gy'=2,'col'=2] {'gx','gy','col'}, use_global_device_ids=true, to_apply=%region_4.5 | all-reduce | flops 6 | bytes 48 | tf_op jit(solution)/shard_map/psum | solution.py:121
  168.1 1.6 fusion.53
  169.8 1.3 fusion.35
  171.0 1.3 fusion.47
  172.3 1.3 fusion.29
  173.6 1.6 fusion.41
  175.3 1.7 fusion.23
  177.0 0.7 subtract_reduce_fusion
  178.1 2.4 %psum.23 = f32[1,4,4]{2,1,0:T(4,128)S(1)} all-reduce(f32[1,4,4]{2,1,0:T(4,128)S(1)} %bitcast.39), channel_id=1, replica_groups=mesh['freq'=2,'gx'=4,'gy'=2,'col'=2] {'col'}, use_global_device_ids=true, to_apply=%region_8.9 | all-reduce | flops 16 | bytes 128 | tf_op jit(solution)/shard_map/psum | solution.py:163
  180.5 26.0 %all_gather.3 = f32[8,4,4]{2,1,0:T(4,128)S(1)} all-gather(f32[1,4,4]{2,1,0:T(4,128)S(1)} %psum.23), channel_id=1, replica_groups=mesh['freq'=2,'gx'=4,'gy'=2,'col'=2] {'gx','gy'}, dimensions={0}, use_global_device_ids=true | all-gather | bytes 576 | tf_op jit(solution)/shard_map/all_gather | solution.py:164
  206.7 0.7 div.40
  207.3 0.9 pad_maximum_fusion.13
  (101 shorter events, 2.3 us)
Async XLA Ops:
  0.6 31.2 %copy-start.33 = (bf16[16,16,128]{2,1,0:T(8,128)(2,1)S(1)}, bf16[16,16,128]{2,1,0:T(8,128)(2,1)}, u32[]{:S(2)}) copy-start(bf16[16,16,128]{2,1,0:T(8,128)(2,1)} %param.12) | copy-start | bytes 196612
  1.4 31.2 %collective-permute-start = (f32[6,1,16,128]{3,2,1,0:T(8,128)S(1)}, f32[6,1,16,128]{3,2,1,0:T(8,128)S(1)}, u32[]{:S(2)}, u32[]{:S(2)}) collective-permute-start(f32[6,1,16,128]{3,2,1,0:T(8,128)S(1)} %get-tuple-element.41), channel_id=1, source_target_pairs={{4,0},{8,4},{12,8},{5,1},{9,5},{13,9},{6,2},{10,6},{14,10},{7,3},{... | collective-permute-start | bytes 147464 | tf_op jit(solution)/shard_map/ppermute | solution.py:18
  2.7 30.0 %collective-permute-start.1 = (f32[6,1,16,128]{3,2,1,0:T(8,128)S(1)}, f32[6,1,16,128]{3,2,1,0:T(8,128)S(1)}, u32[]{:S(2)}, u32[]{:S(2)}) collective-permute-start(f32[6,1,16,128]{3,2,1,0:T(8,128)S(1)} %get-tuple-element.40), channel_id=1, source_target_pairs={{0,4},{4,8},{8,12},{1,5},{5,9},{9,13},{2,6},{6,10},{10,14},{3,7},{... | collective-permute-start | bytes 147464 | tf_op jit(solution)/shard_map/ppermute | solution.py:17
  12.9 19.7 %copy-start.34 = (s32[1,256]{1,0:T(1,128)S(1)}, s32[1,256]{1,0:T(1,128)}, u32[]{:S(2)}) copy-start(s32[1,256]{1,0:T(1,128)} %param.15) | copy-start | bytes 3076
  12.9 19.7 %copy-start.27 = (bf16[6,16,16,128]{3,2,1,0:T(8,128)(2,1)S(1)}, bf16[6,16,16,128]{3,2,1,0:T(8,128)(2,1)}, u32[]{:S(2)}) copy-start(bf16[6,16,16,128]{3,2,1,0:T(8,128)(2,1)} %param.10) | copy-start | bytes 1179652
  31.8 8.1 %copy-start.35 = (f32[2,3]{1,0:T(2,128)S(1)}, f32[2,3]{1,0:T(2,128)}, u32[]{:S(2)}) copy-start(f32[2,3]{1,0:T(2,128)} %param.16) | copy-start | bytes 76
  32.7 9.0 %copy-start.31 = (bf16[6,16,16,128]{3,2,1,0:T(8,128)(2,1)S(1)}, bf16[6,16,16,128]{3,2,1,0:T(8,128)(2,1)}, u32[]{:S(2)}) copy-start(bf16[6,16,16,128]{3,2,1,0:T(8,128)(2,1)} %param.9) | copy-start | bytes 1179652
  32.8 11.9 %collective-permute-start.2 = (f32[6,18,1,128]{3,2,1,0:T(1,128)S(1)}, f32[6,18,1,128]{3,2,1,0:T(1,128)}, u32[]{:S(2)}, u32[]{:S(2)}) collective-permute-start(f32[6,18,1,128]{3,2,1,0:T(1,128)S(1)} %get-tuple-element.35), channel_id=1, source_target_pairs={{2,0},{3,1},{6,4},{7,5},{10,8},{11,9},{14,12},{15,13},{18,16},{19,... | collective-permute-start | bytes 165896 | tf_op jit(solution)/shard_map/ppermute | solution.py:18
  34.1 10.6 %collective-permute-start.3 = (f32[6,18,1,128]{3,2,1,0:T(1,128)S(1)}, f32[6,18,1,128]{3,2,1,0:T(1,128)}, u32[]{:S(2)}, u32[]{:S(2)}) collective-permute-start(f32[6,18,1,128]{3,2,1,0:T(1,128)S(1)} %get-tuple-element.34), channel_id=1, source_target_pairs={{0,2},{1,3},{4,6},{5,7},{8,10},{9,11},{12,14},{13,15},{16,18},{17,... | collective-permute-start | bytes 165896 | tf_op jit(solution)/shard_map/ppermute | solution.py:17
  47.8 8.5 %collective-permute-start.4 = (f32[6,18,18,1]{2,1,3,0:T(8,128)}, f32[6,18,18,1]{2,1,3,0:T(8,128)S(1)}, u32[]{:S(2)}, u32[]{:S(2)}) collective-permute-start(f32[6,18,18,1]{2,1,3,0:T(8,128)} %copy.44), channel_id=1, source_target_pairs={{1,0},{3,2},{5,4},{7,6},{9,8},{11,10},{13,12},{15,14},{17,16},{19,... | collective-permute-start | bytes 23336 | tf_op jit(solution)/shard_map/ppermute | solution.py:18
  50.0 7.0 %collective-permute-start.5 = (f32[6,18,18,1]{2,1,3,0:T(8,128)S(1)}, f32[6,18,18,1]{2,1,3,0:T(8,128)}, u32[]{:S(2)}, u32[]{:S(2)}) collective-permute-start(f32[6,18,18,1]{2,1,3,0:T(8,128)S(1)} %copy.46), channel_id=1, source_target_pairs={{0,1},{2,3},{4,5},{6,7},{8,9},{10,11},{12,13},{14,15},{16,17},{18,... | collective-permute-start | bytes 23336 | tf_op jit(solution)/shard_map/ppermute | solution.py:17
  58.7 3.1 %copy-start.6 = (f32[32768]{0:T(1024)S(1)}, f32[32768]{0:T(1024)}, u32[]{:S(2)}) copy-start(f32[32768]{0:T(1024)} %scatter_custom_fusion) | copy-start | bytes 393220
  58.7 3.1 %copy-start.16 = (f32[6,18,17,128]{3,2,1,0:T(8,128)S(1)}, f32[6,18,17,128]{3,2,1,0:T(8,128)}, u32[]{:S(2)}) copy-start(f32[6,18,17,128]{3,2,1,0:T(8,128)} %get-tuple-element.32) | copy-start | bytes 2820100
  58.7 3.1 %copy-start.17 = (f32[6,18,17,128]{3,2,1,0:T(8,128)S(1)}, f32[6,18,17,128]{3,2,1,0:T(8,128)}, u32[]{:S(2)}) copy-start(f32[6,18,17,128]{3,2,1,0:T(8,128)} %get-tuple-element.33) | copy-start | bytes 2820100
  58.7 3.1 %copy-start.28 = (bf16[6,16,16,128]{3,2,1,0:T(8,128)(2,1)S(1)}, bf16[6,16,16,128]{3,2,1,0:T(8,128)(2,1)}, u32[]{:S(2)}) copy-start(bf16[6,16,16,128]{3,2,1,0:T(8,128)(2,1)} %param.10) | copy-start | bytes 1179652
  93.7 1.6 copy-start
  93.7 1.7 copy-start.20
  95.3 6.1 %copy-start.2 = (f32[1,16,16,128]{3,2,1,0:T(8,128)}, f32[1,16,16,128]{3,2,1,0:T(8,128)S(1)}, u32[]{:S(2)}) copy-start(f32[1,16,16,128]{3,2,1,0:T(8,128)S(1)} %get-tuple-element.15) | copy-start | bytes 393220
  101.4 1.8 copy-start.4
  101.4 1.8 copy-start.7
  101.5 1.8 copy-start.23
  101.5 1.8 copy-start.25
  101.5 1.8 copy-start.29
  104.1 13.9 %copy-start.32 = (bf16[6,16,16,128]{3,2,1,0:T(8,128)(2,1)S(1)}, bf16[6,16,16,128]{3,2,1,0:T(8,128)(2,1)}, u32[]{:S(2)}) copy-start(bf16[6,16,16,128]{3,2,1,0:T(8,128)(2,1)} %param.11) | copy-start | bytes 1179652
  104.1 6.1 %collective-permute-start.6 = (f32[6,1,16,128]{3,2,1,0:T(8,128)S(1)}, f32[6,1,16,128]{3,2,1,0:T(8,128)S(1)}, u32[]{:S(2)}, u32[]{:S(2)}) collective-permute-start(f32[6,1,16,128]{3,2,1,0:T(8,128)S(1)} %get-tuple-element.38), channel_id=1, source_target_pairs={{4,0},{8,4},{12,8},{5,1},{9,5},{13,9},{6,2},{10,6},{14,10},{7,3},{... | collective-permute-start | bytes 147464 | tf_op jit(solution)/shard_map/ppermute | solution.py:18
  105.5 6.3 %collective-permute-start.7 = (f32[6,1,16,128]{3,2,1,0:T(8,128)S(1)}, f32[6,1,16,128]{3,2,1,0:T(8,128)S(1)}, u32[]{:S(2)}, u32[]{:S(2)}) collective-permute-start(f32[6,1,16,128]{3,2,1,0:T(8,128)S(1)} %get-tuple-element.37), channel_id=1, source_target_pairs={{0,4},{4,8},{8,12},{1,5},{5,9},{9,13},{2,6},{6,10},{10,14},{3,7},{... | collective-permute-start | bytes 147464 | tf_op jit(solution)/shard_map/ppermute | solution.py:17
  111.9 7.0 %collective-permute-start.8 = (f32[6,18,1,128]{3,2,1,0:T(1,128)S(1)}, f32[6,18,1,128]{3,2,1,0:T(1,128)S(1)}, u32[]{:S(2)}, u32[]{:S(2)}) collective-permute-start(f32[6,18,1,128]{3,2,1,0:T(1,128)S(1)} %get-tuple-element.31), channel_id=1, source_target_pairs={{2,0},{3,1},{6,4},{7,5},{10,8},{11,9},{14,12},{15,13},{18,16},{19,... | collective-permute-start | bytes 165896 | tf_op jit(solution)/shard_map/ppermute | solution.py:18
  113.2 6.3 %collective-permute-start.9 = (f32[6,18,1,128]{3,2,1,0:T(1,128)S(1)}, f32[6,18,1,128]{3,2,1,0:T(1,128)S(1)}, u32[]{:S(2)}, u32[]{:S(2)}) collective-permute-start(f32[6,18,1,128]{3,2,1,0:T(1,128)S(1)} %get-tuple-element.30), channel_id=1, source_target_pairs={{0,2},{1,3},{4,6},{5,7},{8,10},{9,11},{12,14},{13,15},{16,18},{17,... | collective-permute-start | bytes 165896 | tf_op jit(solution)/shard_map/ppermute | solution.py:17
  118.9 0.6 copy-start.10
  119.6 0.6 copy-start.13
  122.4 6.0 %copy-start.11 = (f32[6,18,1,128]{3,2,1,0:T(1,128)S(1)}, f32[6,18,1,128]{3,2,1,0:T(1,128)}, u32[]{:S(2)}) copy-start(f32[6,18,1,128]{3,2,1,0:T(1,128)} %copy-done.10) | copy-start | bytes 165892
  122.4 6.0 %copy-start.14 = (f32[6,18,1,128]{3,2,1,0:T(1,128)S(1)}, f32[6,18,1,128]{3,2,1,0:T(1,128)}, u32[]{:S(2)}) copy-start(f32[6,18,1,128]{3,2,1,0:T(1,128)} %copy-done.13) | copy-start | bytes 165892
  122.4 7.8 %collective-permute-start.10 = (f32[6,18,18,1]{2,1,3,0:T(8,128)}, f32[6,18,18,1]{2,1,3,0:T(8,128)S(1)}, u32[]{:S(2)}, u32[]{:S(2)}) collective-permute-start(f32[6,18,18,1]{2,1,3,0:T(8,128)} %copy.48), channel_id=1, source_target_pairs={{1,0},{3,2},{5,4},{7,6},{9,8},{11,10},{13,12},{15,14},{17,16},{19,... | collective-permute-start | bytes 23336 | tf_op jit(solution)/shard_map/ppermute | solution.py:18
  124.8 6.2 %collective-permute-start.11 = (f32[6,18,18,1]{2,1,3,0:T(8,128)S(1)}, f32[6,18,18,1]{2,1,3,0:T(8,128)}, u32[]{:S(2)}, u32[]{:S(2)}) collective-permute-start(f32[6,18,18,1]{2,1,3,0:T(8,128)S(1)} %copy.50), channel_id=1, source_target_pairs={{0,1},{2,3},{4,5},{6,7},{8,9},{10,11},{12,13},{14,15},{16,17},{18,... | collective-permute-start | bytes 23336 | tf_op jit(solution)/shard_map/ppermute | solution.py:17
  132.6 3.7 %copy-start.8 = (f32[32768]{0:T(1024)S(1)}, f32[32768]{0:T(1024)}, u32[]{:S(2)}) copy-start(f32[32768]{0:T(1024)} %scatter_custom_fusion) | copy-start | bytes 393220
  132.6 3.7 %copy-start.18 = (f32[6,18,17,128]{3,2,1,0:T(8,128)S(1)}, f32[6,18,17,128]{3,2,1,0:T(8,128)}, u32[]{:S(2)}) copy-start(f32[6,18,17,128]{3,2,1,0:T(8,128)} %get-tuple-element.28) | copy-start | bytes 2820100
  132.6 3.7 %copy-start.19 = (f32[6,18,17,128]{3,2,1,0:T(8,128)S(1)}, f32[6,18,17,128]{3,2,1,0:T(8,128)}, u32[]{:S(2)}) copy-start(f32[6,18,17,128]{3,2,1,0:T(8,128)} %get-tuple-element.29) | copy-start | bytes 2820100
  168.1 1.6 copy-start.1
  168.1 1.6 copy-start.3
  168.1 1.6 copy-start.12
  168.1 1.6 copy-start.15
  168.1 1.6 copy-start.22
  175.2 1.8 copy-start.5
  175.2 1.8 copy-start.9
  175.2 1.8 copy-start.21
  175.2 1.8 copy-start.24
  175.3 1.8 copy-start.26
  175.3 1.8 copy-start.30
where the time goes:
time: 210 us; the launch traced here: 208 us
  blocking collectives  87.4 us (42%)
  other arithmetic  61.2 us (29%)
  starting transfers between devices  35.9 us (17%)
  local copies, waits for them, and re-layouts  19.4 us (9%)
  waiting for transfers between devices  2.4 us (1%)
    psum x2, blocking collectives, foundation(): total = lax.psum(jnp.sum(mask * field, axis=(1, 2, 3)), ('gx', 'gy', 'col'))  58.9 us
    ppermute x6, starting transfers between devices, with_halo(): before = lax.ppermute(last, axis, up)  27.9 us
    all_gather x1, blocking collectives, shards(): gathered = lax.all_gather(paired[None], ('gx', 'gy'), axis=0, tiled=True)  26 us
    add x12, other arithmetic, navier(): result.append(shear * laplace[channel] + (lame_first + shear) * divergence)  18.1 us
    concatenate x8, other arithmetic, with_halo(): array = jnp.concatenate([before, array, after], axis=dim)  12.4 us
    add x1, other arithmetic, sweep(): diag_real = 8.0 * shear + 2.0 * lame_first - inertia + mask * imp_real  8.89 us
    ppermute x6, starting transfers between devices, with_halo(): after = lax.ppermute(initial, axis, down)  7.99 us
    select_n x2, other arithmetic, material(): lame_first = jnp.where(chosen, table[entry, 0], lame_first)  6.44 us
  transfers between devices with their start and end apart: 12, of which 3 were waited for; matrix products, arithmetic and copies ran while one was open for 18% of the time, Pallas kernels for 0%

commit v1 on v0

--- a/solution.py
+++ b/solution.py
@@ -5,6 +5,12 @@
 
 DAMPING = 0.5
 RELAXATION = 0.6
+
+
+def add_all(shard, mesh_axis):
+    terms = lax.all_gather(shard, mesh_axis, axis=0, tiled=False)
+    total = terms.sum(axis=0)
+    return total
 
 
 def with_halo(array, sides, width):
@@ -118,7 +124,7 @@
 
 
 def foundation(field, mask, count):
-    total = lax.psum(jnp.sum(mask * field, axis=(1, 2, 3)), ("gx", "gy", "col"))
+    total = add_all(jnp.sum(mask * field, axis=(1, 2, 3)), ("gx", "gy", "col"))
     return total / count
 
 

time: 210 us -> 216 us (1.029)
  local copies, waits for them, and re-layouts: 19.4 us -> 21.9 us
  other arithmetic: 61.2 us -> 63.6 us
    unnamed x0 -> x2, blocking collectives: none -> 60 us
    psum x2 -> x0, blocking collectives: 58.9 us -> none  [foundation(): total = lax.psum(jnp.sum(mask * field, axis=(1, 2, 3)), ('gx', 'gy', 'col'))]
  transfers between devices with their start and end apart: 12 -> 12, of which waited for: 3 -> 2; matrix products, arithmetic and copies ran while one was open for 18% -> 17% of each run, Pallas kernels for 0% -> 0%
where the time goes in v1:
time: 216 us; the launch traced here: 215 us
  blocking collectives  88.4 us (41%)
  other arithmetic  63.6 us (29%)
  starting transfers between devices  35.9 us (17%)
  local copies, waits for them, and re-layouts  21.9 us (10%)
  between operations  2.67 us (1%)
  waiting for transfers between devices  2.39 us (1%)
    unnamed x2, blocking collectives  60 us
    ppermute x6, starting transfers between devices, with_halo(): before = lax.ppermute(last, axis, up)  27.9 us
    all_gather x1, blocking collectives, shards(): gathered = lax.all_gather(paired[None], ('gx', 'gy'), axis=0, tiled=True)  26 us
    add x12, other arithmetic, navier(): result.append(shear * laplace[channel] + (lame_first + shear) * divergence)  18.2 us
    concatenate x8, other arithmetic, with_halo(): array = jnp.concatenate([before, array, after], axis=dim)  12.4 us
    add x1, other arithmetic, sweep(): diag_real = 8.0 * shear + 2.0 * lame_first - inertia + mask * imp_real  8.8 us
    ppermute x6, starting transfers between devices, with_halo(): after = lax.ppermute(initial, axis, down)  7.99 us
    select_n x2, other arithmetic, material(): lame_first = jnp.where(chosen, table[entry, 0], lame_first)  6.47 us
  transfers between devices with their start and end apart: 12, of which 2 were waited for; matrix products, arithmetic and copies ran while one was open for 17% of the time, Pallas kernels for 0%

profile of v1, /device:TPU:0, one launch (start us, length us, event | category | flops | bytes accessed | tf_op | source)
XLA Modules:
  0.0 214.9 jit_solution(547567721432669373)
XLA Ops:
  0.6 0.8 fusion.107
  1.4 1.3 collective-permute-start
  2.7 5.6 %collective-permute-start.1 = (f32[6,1,16,128]{3,2,1,0:T(8,128)S(1)}, f32[6,1,16,128]{3,2,1,0:T(8,128)S(1)}, u32[]{:S(2)}, u32[]{:S(2)}) collective-permute-start(f32[6,1,16,128]{3,2,1,0:T(8,128)S(1)} %get-tuple-element.40), channel_id=1, source_target_pairs={{0,4},{4,8},{8,12},{1,5},{5,9},{9,13},{2,6},{6,10},{10,14},{3,7},{... | collective-permute-start | bytes 147464 | tf_op jit(solution)/shard_map/ppermute | solution.py:23
  8.3 2.0 fusion.108
  10.3 0.7 broadcast_compare_fusion.7
  11.0 1.9 broadcast_select_fusion
  12.9 4.5 %select_select_fusion.1 = f32[2,8,2,8,4,32]{5,4,3,2,1,0:T(4,128)S(1)} fusion(f32[]{:T(128)} %bitcast, f32[]{:T(128)} %bitcast.1, f32[]{:T(128)} %bitcast.2, f32[]{:T(128)} %bitcast.3, f32[]{:T(128)} %bitcast.4, f32[2,2,4]{2,1,0:T(2,128)S(1)} %get-tuple-element.46, f32[]{:T(128)} %bitcast.6, f32[]{:T(128)} %bitcast.5, ...), kind=kLoop, calls=%fused_computation.41 | loop fusion | flops 229376 | bytes 131276 | tf_op jit(solution)/shard_map/jit(_where)/select_n | solution.py:122
  17.4 4.5 %select_select_fusion = f32[2,8,2,8,4,32]{5,4,3,2,1,0:T(4,128)S(1)} fusion(f32[]{:T(128)} %bitcast.8, f32[]{:T(128)} %bitcast.9, f32[]{:T(128)} %bitcast.10, f32[]{:T(128)} %bitcast.11, f32[]{:T(128)} %bitcast.12, f32[2,2,4]{2,1,0:T(2,128)S(1)} %get-tuple-element.45, f32[]{:T(128)} %bitcast.14, f32[]{:T(128)} %bitcast.13, ...), kind=kLoop, calls=%fused_computation.40 | loop fusion | flops 229376 | bytes 131276 | tf_op jit(solution)/shard_map/jit(_where)/select_n | solution.py:121
  21.9 8.8 %multiply_add_fusion = f32[2,8,2,8,4,32]{5,4,3,2,1,0:T(4,128)S(1)} fusion(f32[2,2,4]{2,1,0:T(2,128)S(1)} %get-tuple-element.46, f32[]{:T(128)} %bitcast.6, pred[2,2,4]{2,1,0:T(4,128)(4,1)S(1)} %get-tuple-element.53, f32[]{:T(128)} %bitcast.5, pred[2,2,4]{2,1,0:T(4,128)(4,1)S(1)} %get-tuple-element.48, f32[]{:T(128)} %bitcast.4, ...), kind=kLoop, calls=%fused_computation.39 | loop fusion | flops 557056 | bytes 131368 | tf_op jit(solution)/shard_map/add | solution.py:100
  31.7 0.8 convert_multiply_fusion
  32.7 1.3 collective-permute-start.2
  34.0 5.8 %collective-permute-start.3 = (f32[6,18,1,128]{3,2,1,0:T(1,128)S(1)}, f32[6,18,1,128]{3,2,1,0:T(1,128)}, u32[]{:S(2)}, u32[]{:S(2)}) collective-permute-start(f32[6,18,1,128]{3,2,1,0:T(1,128)S(1)} %get-tuple-element.34), channel_id=1, source_target_pairs={{0,2},{1,3},{4,6},{5,7},{8,10},{9,11},{12,14},{13,15},{16,18},{17,... | collective-permute-start | bytes 165896 | tf_op jit(solution)/shard_map/ppermute | solution.py:23
  39.8 0.9 reshape.315
  40.7 0.9 reshape.317
  41.6 1.0 convert_element_type.13
  43.8 2.0 scatter_custom_fusion
  45.9 1.0 pad_maximum_fusion.3
  47.3 1.6 copy.44
  48.9 1.3 collective-permute-start.4
  50.2 0.9 copy.46
  51.1 3.7 %collective-permute-start.5 = (f32[6,18,18,1]{2,1,3,0:T(8,128)S(1)}, f32[6,18,18,1]{2,1,3,0:T(8,128)}, u32[]{:S(2)}, u32[]{:S(2)}) collective-permute-start(f32[6,18,18,1]{2,1,3,0:T(8,128)S(1)} %copy.46), channel_id=1, source_target_pairs={{0,1},{2,3},{4,5},{6,7},{8,9},{10,11},{12,13},{14,15},{16,17},{18,... | collective-permute-start | bytes 23336 | tf_op jit(solution)/shard_map/ppermute | solution.py:23
  54.8 2.5 %pad_maximum_fusion.2 = (f32[6,18,17,128]{3,2,1,0:T(8,128)}, f32[6,18,17,128]{3,2,1,0:T(8,128)}) fusion(f32[6,18,1,128]{3,2,1,0:T(1,128)} %collective-permute-done.2, f32[6,1,16,128]{3,2,1,0:T(8,128)S(1)} %collective-permute-done, f32[6,16,16,128]{3,2,1,0:T(8,128)S(1)} %convert_element_type.12, f32[6,1,16,128]{3,2,1,0:T(8,128)S(1)} %collective-permute-done.1, ...), kind=kLoop, calls=%fused_computation.5 | loop fusion | flops 1410048 | bytes 2875392 | tf_op jit(solution)/shard_map/concatenate | solution.py:25
  57.3 0.8 copy.45
  58.1 1.7 copy.47
  59.8 3.1 %pad_maximum_fusion = (f32[6,18,18,129]{3,2,1,0:T(8,128)S(1)}, f32[6,18,18,129]{3,2,1,0:T(8,128)S(1)}) fusion(f32[6,18,18,1]{3,2,1,0:T(8,128)S(1)} %copy.45, f32[6,18,1,128]{3,2,1,0:T(1,128)} %collective-permute-done.2, f32[6,1,16,128]{3,2,1,0:T(8,128)S(1)} %collective-permute-done, f32[6,16,16,128]{3,2,1,0:T(8,128)S(1)} %convert_element_type.12, ...), kind=kLoop, calls=%fused_computation.1 | loop fusion | flops 2507760 | bytes 3017088 | tf_op jit(solution)/shard_map/concatenate | solution.py:25
  62.9 2.3 %add_add_fusion.1 = (f32[6,16,16,128]{3,2,1,0:T(8,128)}, f32[6,16,16,128]{3,2,1,0:T(8,128)}, f32[6,16,16,128]{3,2,1,0:T(8,128)}, f32[6,16,16,128]{3,2,1,0:T(8,128)}, f32[6]{0:T(128)S(1)}) fusion(bf16[6,16,16,128]{3,2,1,0:T(8,128)(2,1)S(1)} %copy-done.28, f32[6,18,17,128]{3,2,1,0:T(8,128)S(1)} %copy-done.17, f32[6,18,17,128]{3,2,1,0:T(8,128)S(1)} %copy-done.16, ...), kind=kLoop, calls=%fused_computation.38 | loop fusion | flops 2949114 | bytes 7700504 | tf_op jit(solution)/shard_map/add | solution.py:49
  65.4 30.0 %all-reduce = f32[96]{0:T(128)} all-reduce(f32[96]{0:T(128)S(1)} %dynamic-update-slice), channel_id=2, replica_groups=mesh['freq'=2,'gx'=4,'gy'=2,'col'=2] {'gx','gy','col'}, use_global_device_ids=true, to_apply=%add | all-reduce | flops 96 | bytes 768
  95.5 0.7 reshape.312
  96.8 0.7 broadcast_multiply_fusion.2
  97.6 1.6 fusion.71
  99.2 1.4 fusion.89
  100.7 1.4 fusion.83
  102.1 1.6 fusion.65
  103.7 1.7 fusion.77
  105.5 1.7 fusion.59
  108.1 1.4 collective-permute-start.6
  109.5 4.7 %collective-permute-start.7 = (f32[6,1,16,128]{3,2,1,0:T(8,128)S(1)}, f32[6,1,16,128]{3,2,1,0:T(8,128)S(1)}, u32[]{:S(2)}, u32[]{:S(2)}) collective-permute-start(f32[6,1,16,128]{3,2,1,0:T(8,128)S(1)} %get-tuple-element.37), channel_id=1, source_target_pairs={{0,4},{4,8},{8,12},{1,5},{5,9},{9,13},{2,6},{6,10},{10,14},{3,7},{... | collective-permute-start | bytes 147464 | tf_op jit(solution)/shard_map/ppermute | solution.py:23
  114.3 1.5 collective-permute-done.7
  115.9 1.3 collective-permute-start.8
  117.2 4.5 %collective-permute-start.9 = (f32[6,18,1,128]{3,2,1,0:T(1,128)S(1)}, f32[6,18,1,128]{3,2,1,0:T(1,128)S(1)}, u32[]{:S(2)}, u32[]{:S(2)}) collective-permute-start(f32[6,18,1,128]{3,2,1,0:T(1,128)S(1)} %get-tuple-element.30), channel_id=1, source_target_pairs={{0,2},{1,3},{4,6},{5,7},{8,10},{9,11},{12,14},{13,15},{16,18},{17,... | collective-permute-start | bytes 165896 | tf_op jit(solution)/shard_map/ppermute | solution.py:23
  121.8 1.0 convert_element_type.15
  122.7 0.8 collective-permute-done.9
  124.8 1.6 copy.48
  126.4 1.4 collective-permute-start.10
  127.8 0.9 copy.50
  128.7 3.7 %collective-permute-start.11 = (f32[6,18,18,1]{2,1,3,0:T(8,128)S(1)}, f32[6,18,18,1]{2,1,3,0:T(8,128)}, u32[]{:S(2)}, u32[]{:S(2)}) collective-permute-start(f32[6,18,18,1]{2,1,3,0:T(8,128)S(1)} %copy.50), channel_id=1, source_target_pairs={{0,1},{2,3},{4,5},{6,7},{8,9},{10,11},{12,13},{14,15},{16,17},{18,... | collective-permute-start | bytes 23336 | tf_op jit(solution)/shard_map/ppermute | solution.py:23
  132.4 1.7 pad_maximum_fusion.4
  134.1 0.8 copy.49
  134.9 1.7 copy.51
  136.6 3.6 %pad_maximum_fusion.1 = (f32[6,18,18,129]{3,2,1,0:T(8,128)S(1)}, f32[6,18,18,129]{3,2,1,0:T(8,128)S(1)}) fusion(f32[6,18,18,1]{3,2,1,0:T(8,128)S(1)} %copy.49, f32[6,18,1,128]{3,2,1,0:T(1,128)} %copy-done.10, f32[6,1,16,128]{3,2,1,0:T(8,128)S(1)} %collective-permute-done.6, f32[3,16,16,128]{3,2,1,0:T(8,128)S(1)} %divide_add_fusion.2, ...), kind=kLoop, calls=%fused_computation.3 | loop fusion | flops 3009312 | bytes 3017088 | tf_op jit(solution)/shard_map/concatenate | solution.py:25
  140.2 2.3 %add_add_fusion = (f32[6,16,16,128]{3,2,1,0:T(8,128)}, f32[6,16,16,128]{3,2,1,0:T(8,128)}, f32[6,16,16,128]{3,2,1,0:T(8,128)}, f32[6,16,16,128]{3,2,1,0:T(8,128)}, f32[6]{0:T(128)S(1)}) fusion(f32[3,16,16,128]{3,2,1,0:T(8,128)S(1)} %divide_add_fusion.2, f32[3,16,16,128]{3,2,1,0:T(8,128)S(1)} %get-tuple-element.11, f32[6,18,17,128]{3,2,1,0:T(8,128)S(1)} %copy-done.19, ...), kind=kLoop, calls=%fused_computation.36 | loop fusion | flops 3145722 | bytes 7307288 | tf_op jit(solution)/shard_map/add | solution.py:49
  142.7 30.0 %all-reduce.1 = f32[96]{0:T(128)} all-reduce(f32[96]{0:T(128)S(1)} %dynamic-update-slice.1), channel_id=3, replica_groups=mesh['freq'=2,'gx'=4,'gy'=2,'col'=2] {'gx','gy','col'}, use_global_device_ids=true, to_apply=%add.1 | all-reduce | flops 96 | bytes 768
  172.7 0.7 reshape.313
  174.7 1.6 fusion.53
  176.4 1.3 fusion.35
  177.6 1.3 fusion.47
  178.9 1.3 fusion.29
  180.2 1.6 fusion.41
  181.9 1.7 fusion.23
  183.6 0.7 subtract_reduce_fusion
  184.7 2.4 %psum.7 = f32[1,4,4]{2,1,0:T(4,128)S(1)} all-reduce(f32[1,4,4]{2,1,0:T(4,128)S(1)} %bitcast.40), channel_id=1, replica_groups=mesh['freq'=2,'gx'=4,'gy'=2,'col'=2] {'col'}, use_global_device_ids=true, to_apply=%region_8.9 | all-reduce | flops 16 | bytes 128 | tf_op jit(solution)/shard_map/psum | solution.py:169
  187.1 26.0 %all_gather.19 = f32[8,4,4]{2,1,0:T(4,128)S(1)} all-gather(f32[1,4,4]{2,1,0:T(4,128)S(1)} %psum.7), channel_id=1, replica_groups=mesh['freq'=2,'gx'=4,'gy'=2,'col'=2] {'gx','gy'}, dimensions={0}, use_global_device_ids=true | all-gather | bytes 576 | tf_op jit(solution)/shard_map/all_gather | solution.py:170
  213.3 0.7 div.40
  213.9 0.9 pad_maximum_fusion.13
  (112 shorter events, 6.5 us)
Async XLA Ops:
  0.6 31.0 %copy-start.33 = (bf16[16,16,128]{2,1,0:T(8,128)(2,1)S(1)}, bf16[16,16,128]{2,1,0:T(8,128)(2,1)}, u32[]{:S(2)}) copy-start(bf16[16,16,128]{2,1,0:T(8,128)(2,1)} %param.12) | copy-start | bytes 196612
  1.4 31.1 %collective-permute-start = (f32[6,1,16,128]{3,2,1,0:T(8,128)S(1)}, f32[6,1,16,128]{3,2,1,0:T(8,128)S(1)}, u32[]{:S(2)}, u32[]{:S(2)}) collective-permute-start(f32[6,1,16,128]{3,2,1,0:T(8,128)S(1)} %get-tuple-element.41), channel_id=1, source_target_pairs={{4,0},{8,4},{12,8},{5,1},{9,5},{13,9},{6,2},{10,6},{14,10},{7,3},{... | collective-permute-start | bytes 147464 | tf_op jit(solution)/shard_map/ppermute | solution.py:24
  2.7 29.8 %collective-permute-start.1 = (f32[6,1,16,128]{3,2,1,0:T(8,128)S(1)}, f32[6,1,16,128]{3,2,1,0:T(8,128)S(1)}, u32[]{:S(2)}, u32[]{:S(2)}) collective-permute-start(f32[6,1,16,128]{3,2,1,0:T(8,128)S(1)} %get-tuple-element.40), channel_id=1, source_target_pairs={{0,4},{4,8},{8,12},{1,5},{5,9},{9,13},{2,6},{6,10},{10,14},{3,7},{... | collective-permute-start | bytes 147464 | tf_op jit(solution)/shard_map/ppermute | solution.py:23
  12.9 19.5 %copy-start.34 = (s32[1,256]{1,0:T(1,128)S(1)}, s32[1,256]{1,0:T(1,128)}, u32[]{:S(2)}) copy-start(s32[1,256]{1,0:T(1,128)} %param.15) | copy-start | bytes 3076
  12.9 19.5 %copy-start.27 = (bf16[6,16,16,128]{3,2,1,0:T(8,128)(2,1)S(1)}, bf16[6,16,16,128]{3,2,1,0:T(8,128)(2,1)}, u32[]{:S(2)}) copy-start(bf16[6,16,16,128]{3,2,1,0:T(8,128)(2,1)} %param.10) | copy-start | bytes 1179652
  31.7 8.1 %copy-start.35 = (f32[2,3]{1,0:T(2,128)S(1)}, f32[2,3]{1,0:T(2,128)}, u32[]{:S(2)}) copy-start(f32[2,3]{1,0:T(2,128)} %param.16) | copy-start | bytes 76
  32.5 9.0 %copy-start.31 = (bf16[6,16,16,128]{3,2,1,0:T(8,128)(2,1)S(1)}, bf16[6,16,16,128]{3,2,1,0:T(8,128)(2,1)}, u32[]{:S(2)}) copy-start(bf16[6,16,16,128]{3,2,1,0:T(8,128)(2,1)} %param.9) | copy-start | bytes 1179652
  32.7 9.9 %copy-start.36 = (u32[32]{0:T(128)S(1)}, u32[32]{0:T(128)}, u32[]{:S(2)}) copy-start(u32[32]{0:T(128)} %constant.50) | copy-start | bytes 388
  32.7 13.2 %collective-permute-start.2 = (f32[6,18,1,128]{3,2,1,0:T(1,128)S(1)}, f32[6,18,1,128]{3,2,1,0:T(1,128)}, u32[]{:S(2)}, u32[]{:S(2)}) collective-permute-start(f32[6,18,1,128]{3,2,1,0:T(1,128)S(1)} %get-tuple-element.35), channel_id=1, source_target_pairs={{2,0},{3,1},{6,4},{7,5},{10,8},{11,9},{14,12},{15,13},{18,16},{19,... | collective-permute-start | bytes 165896 | tf_op jit(solution)/shard_map/ppermute | solution.py:24
  34.0 11.9 %collective-permute-start.3 = (f32[6,18,1,128]{3,2,1,0:T(1,128)S(1)}, f32[6,18,1,128]{3,2,1,0:T(1,128)}, u32[]{:S(2)}, u32[]{:S(2)}) collective-permute-start(f32[6,18,1,128]{3,2,1,0:T(1,128)S(1)} %get-tuple-element.34), channel_id=1, source_target_pairs={{0,2},{1,3},{4,6},{5,7},{8,10},{9,11},{12,14},{13,15},{16,18},{17,... | collective-permute-start | bytes 165896 | tf_op jit(solution)/shard_map/ppermute | solution.py:23
  48.9 8.4 %collective-permute-start.4 = (f32[6,18,18,1]{2,1,3,0:T(8,128)}, f32[6,18,18,1]{2,1,3,0:T(8,128)S(1)}, u32[]{:S(2)}, u32[]{:S(2)}) collective-permute-start(f32[6,18,18,1]{2,1,3,0:T(8,128)} %copy.44), channel_id=1, source_target_pairs={{1,0},{3,2},{5,4},{7,6},{9,8},{11,10},{13,12},{15,14},{17,16},{19,... | collective-permute-start | bytes 23336 | tf_op jit(solution)/shard_map/ppermute | solution.py:24
  51.1 7.0 %collective-permute-start.5 = (f32[6,18,18,1]{2,1,3,0:T(8,128)S(1)}, f32[6,18,18,1]{2,1,3,0:T(8,128)}, u32[]{:S(2)}, u32[]{:S(2)}) collective-permute-start(f32[6,18,18,1]{2,1,3,0:T(8,128)S(1)} %copy.46), channel_id=1, source_target_pairs={{0,1},{2,3},{4,5},{6,7},{8,9},{10,11},{12,13},{14,15},{16,17},{18,... | collective-permute-start | bytes 23336 | tf_op jit(solution)/shard_map/ppermute | solution.py:23
  59.8 3.1 %copy-start.6 = (f32[32768]{0:T(1024)S(1)}, f32[32768]{0:T(1024)}, u32[]{:S(2)}) copy-start(f32[32768]{0:T(1024)} %scatter_custom_fusion) | copy-start | bytes 393220
  59.8 3.1 %copy-start.16 = (f32[6,18,17,128]{3,2,1,0:T(8,128)S(1)}, f32[6,18,17,128]{3,2,1,0:T(8,128)}, u32[]{:S(2)}) copy-start(f32[6,18,17,128]{3,2,1,0:T(8,128)} %get-tuple-element.32) | copy-start | bytes 2820100
  59.8 3.1 %copy-start.17 = (f32[6,18,17,128]{3,2,1,0:T(8,128)S(1)}, f32[6,18,17,128]{3,2,1,0:T(8,128)}, u32[]{:S(2)}) copy-start(f32[6,18,17,128]{3,2,1,0:T(8,128)} %get-tuple-element.33) | copy-start | bytes 2820100
  59.8 3.1 %copy-start.28 = (bf16[6,16,16,128]{3,2,1,0:T(8,128)(2,1)S(1)}, bf16[6,16,16,128]{3,2,1,0:T(8,128)(2,1)}, u32[]{:S(2)}) copy-start(bf16[6,16,16,128]{3,2,1,0:T(8,128)(2,1)} %param.10) | copy-start | bytes 1179652
  97.6 1.6 copy-start
  97.6 1.7 copy-start.20
  99.2 6.2 %copy-start.2 = (f32[1,16,16,128]{3,2,1,0:T(8,128)}, f32[1,16,16,128]{3,2,1,0:T(8,128)S(1)}, u32[]{:S(2)}) copy-start(f32[1,16,16,128]{3,2,1,0:T(8,128)S(1)} %get-tuple-element.15) | copy-start | bytes 393220
  105.4 1.8 copy-start.4
  105.4 1.8 copy-start.7
  105.4 1.8 copy-start.23
  105.5 1.8 copy-start.25
  105.5 1.8 copy-start.29
  108.1 13.7 %copy-start.32 = (bf16[6,16,16,128]{3,2,1,0:T(8,128)(2,1)S(1)}, bf16[6,16,16,128]{3,2,1,0:T(8,128)(2,1)}, u32[]{:S(2)}) copy-start(bf16[6,16,16,128]{3,2,1,0:T(8,128)(2,1)} %param.11) | copy-start | bytes 1179652
  108.1 6.2 %collective-permute-start.6 = (f32[6,1,16,128]{3,2,1,0:T(8,128)S(1)}, f32[6,1,16,128]{3,2,1,0:T(8,128)S(1)}, u32[]{:S(2)}, u32[]{:S(2)}) collective-permute-start(f32[6,1,16,128]{3,2,1,0:T(8,128)S(1)} %get-tuple-element.38), channel_id=1, source_target_pairs={{4,0},{8,4},{12,8},{5,1},{9,5},{13,9},{6,2},{10,6},{14,10},{7,3},{... | collective-permute-start | bytes 147464 | tf_op jit(solution)/shard_map/ppermute | solution.py:24
  109.5 6.3 %collective-permute-start.7 = (f32[6,1,16,128]{3,2,1,0:T(8,128)S(1)}, f32[6,1,16,128]{3,2,1,0:T(8,128)S(1)}, u32[]{:S(2)}, u32[]{:S(2)}) collective-permute-start(f32[6,1,16,128]{3,2,1,0:T(8,128)S(1)} %get-tuple-element.37), channel_id=1, source_target_pairs={{0,4},{4,8},{8,12},{1,5},{5,9},{9,13},{2,6},{6,10},{10,14},{3,7},{... | collective-permute-start | bytes 147464 | tf_op jit(solution)/shard_map/ppermute | solution.py:23
  115.9 6.8 %collective-permute-start.8 = (f32[6,18,1,128]{3,2,1,0:T(1,128)S(1)}, f32[6,18,1,128]{3,2,1,0:T(1,128)S(1)}, u32[]{:S(2)}, u32[]{:S(2)}) collective-permute-start(f32[6,18,1,128]{3,2,1,0:T(1,128)S(1)} %get-tuple-element.31), channel_id=1, source_target_pairs={{2,0},{3,1},{6,4},{7,5},{10,8},{11,9},{14,12},{15,13},{18,16},{19,... | collective-permute-start | bytes 165896 | tf_op jit(solution)/shard_map/ppermute | solution.py:24
  117.2 6.3 %collective-permute-start.9 = (f32[6,18,1,128]{3,2,1,0:T(1,128)S(1)}, f32[6,18,1,128]{3,2,1,0:T(1,128)S(1)}, u32[]{:S(2)}, u32[]{:S(2)}) collective-permute-start(f32[6,18,1,128]{3,2,1,0:T(1,128)S(1)} %get-tuple-element.30), channel_id=1, source_target_pairs={{0,2},{1,3},{4,6},{5,7},{8,10},{9,11},{12,14},{13,15},{16,18},{17,... | collective-permute-start | bytes 165896 | tf_op jit(solution)/shard_map/ppermute | solution.py:23
  122.7 0.8 copy-start.10
  123.6 0.6 copy-start.13
  126.4 6.0 %copy-start.11 = (f32[6,18,1,128]{3,2,1,0:T(1,128)S(1)}, f32[6,18,1,128]{3,2,1,0:T(1,128)}, u32[]{:S(2)}) copy-start(f32[6,18,1,128]{3,2,1,0:T(1,128)} %copy-done.10) | copy-start | bytes 165892
  126.4 6.0 %copy-start.14 = (f32[6,18,1,128]{3,2,1,0:T(1,128)S(1)}, f32[6,18,1,128]{3,2,1,0:T(1,128)}, u32[]{:S(2)}) copy-start(f32[6,18,1,128]{3,2,1,0:T(1,128)} %copy-done.13) | copy-start | bytes 165892
  126.4 7.8 %collective-permute-start.10 = (f32[6,18,18,1]{2,1,3,0:T(8,128)}, f32[6,18,18,1]{2,1,3,0:T(8,128)S(1)}, u32[]{:S(2)}, u32[]{:S(2)}) collective-permute-start(f32[6,18,18,1]{2,1,3,0:T(8,128)} %copy.48), channel_id=1, source_target_pairs={{1,0},{3,2},{5,4},{7,6},{9,8},{11,10},{13,12},{15,14},{17,16},{19,... | collective-permute-start | bytes 23336 | tf_op jit(solution)/shard_map/ppermute | solution.py:24
  128.7 6.2 %collective-permute-start.11 = (f32[6,18,18,1]{2,1,3,0:T(8,128)S(1)}, f32[6,18,18,1]{2,1,3,0:T(8,128)}, u32[]{:S(2)}, u32[]{:S(2)}) collective-permute-start(f32[6,18,18,1]{2,1,3,0:T(8,128)S(1)} %copy.50), channel_id=1, source_target_pairs={{0,1},{2,3},{4,5},{6,7},{8,9},{10,11},{12,13},{14,15},{16,17},{18,... | collective-permute-start | bytes 23336 | tf_op jit(solution)/shard_map/ppermute | solution.py:23
  136.6 3.7 %copy-start.8 = (f32[32768]{0:T(1024)S(1)}, f32[32768]{0:T(1024)}, u32[]{:S(2)}) copy-start(f32[32768]{0:T(1024)} %scatter_custom_fusion) | copy-start | bytes 393220
  136.6 3.7 %copy-start.18 = (f32[6,18,17,128]{3,2,1,0:T(8,128)S(1)}, f32[6,18,17,128]{3,2,1,0:T(8,128)}, u32[]{:S(2)}) copy-start(f32[6,18,17,128]{3,2,1,0:T(8,128)} %get-tuple-element.28) | copy-start | bytes 2820100
  136.6 3.7 %copy-start.19 = (f32[6,18,17,128]{3,2,1,0:T(8,128)S(1)}, f32[6,18,17,128]{3,2,1,0:T(8,128)}, u32[]{:S(2)}) copy-start(f32[6,18,17,128]{3,2,1,0:T(8,128)} %get-tuple-element.29) | copy-start | bytes 2820100
  174.7 1.6 copy-start.1
  174.7 1.6 copy-start.3
  174.7 1.6 copy-start.12
  174.7 1.6 copy-start.15
  174.7 1.6 copy-start.22
  181.8 1.8 copy-start.5
  181.8 1.8 copy-start.9
  181.8 1.8 copy-start.21
  181.8 1.8 copy-start.24
  181.8 1.8 copy-start.26
  181.9 1.8 copy-start.30
